TPU v7x, 32 devices: a whole 2x2x4 slice. The times are simulated.
32 devices in a mesh: sub: 8 (over z, x), grp: 4 (over y, core).
Axes of the slice: x: 2, y: 2, z: 4, core: 2. Of those that a mesh axis runs over, the one named last changes fastest.
Arguments:
- resid: float32 [32768, 256], P(('sub', 'grp')), may hold values from -6 to 6
- schur_inv: bfloat16 [65536, 2048], P(('sub', 'grp')), may hold values from -0.125 to 0.125
- basis: bfloat16 [512, 2048], P(('sub', 'grp')), may hold values from -1.5 to 1.5
- scaling: float32 [65536], P(('sub', 'grp')), may hold values from 0.25 to 1
- coarse_inv: bfloat16 [512, 512], P(('sub', 'grp')), may hold values from -0.5 to 0.5
- source_row: int32 [65536], P(('sub', 'grp')), may hold values from 0 to 3071, as said below
- primal_idx: int32 [512], P(('sub', 'grp')), may hold values from 0 to 2047, as said below
Outputs:
- first_apply: float32 [32768, 256], P(('sub', 'grp'))
- second_apply: float32 [32768, 256], P(('sub', 'grp'))
Inputs may be any that keep to these rules, and one draw needn't show every extreme that they name: `source_row`: within one subdomain the entries are distinct; the first subdomain of each chain has none below 1024, the last none at or above 2048. `primal_idx`: within one subdomain the entries are distinct.
All inputs are finite; a program needn't handle non-finite values.
Results may differ from a plain program's by a relative error of at most 0.0076.
Values may be sent and summed in bfloat16 or wider, within the bound.
No kernel may reach another device: no remote copies, remote signals or barrier semaphores. Data moves between devices by JAX's collectives and lax.ppermute only.
A program may use at most 64 MiB of HBM per device.

v0:
```python
import jax
import jax.numpy as jnp
from jax import lax
from jax.sharding import PartitionSpec as P


def with_halo(cells, sides, width):
    for axis, dim in sides:
        count = lax.axis_size(axis)
        ends = count - 1
        head = lax.slice_in_dim(cells, 0, width, axis=dim)
        tail = lax.slice_in_dim(cells, cells.shape[dim] - width, cells.shape[dim], axis=dim)
        cells = jnp.concatenate(
            [
                lax.ppermute(tail, axis, [(i, (i + 1) % count) for i in range(ends)]),
                cells,
                lax.ppermute(head, axis, [((i + 1) % count, i) for i in range(ends)]),
            ],
            axis=dim,
        )
    return cells


def shifted(shard, axis, by):
    devices = lax.axis_size(axis)
    pairs = [(i, i + by) for i in range(devices) if 0 <= i + by < devices]
    return lax.ppermute(shard, axis, pairs)


def shards(resid, schur_inv, basis, scaling, coarse_inv, source_row, primal_idx):
    own_count = resid.shape[0]
    scale_column = scaling[:, None]

    def add_all(portion):
        return jnp.dot(coarse_inv, portion, preferred_element_type=jnp.float32)

    def precondition(vector_in):
        rounded = vector_in.astype(jnp.bfloat16)
        padded = with_halo(rounded, (("sub", 0),), own_count)
        gathered = padded[source_row]
        scaled = (scale_column * gathered.astype(jnp.float32)).astype(jnp.bfloat16)
        primal = scaled[primal_idx]
        idx = lax.axis_index("sub") * lax.axis_size("grp") + lax.axis_index("grp")
        total = lax.axis_size("sub") * lax.axis_size("grp") * primal.shape[0]
        buf = lax.dynamic_update_slice(
            jnp.zeros((total, primal.shape[1]), primal.dtype), primal, (idx * primal.shape[0], 0)
        )
        coarse = add_all(lax.psum(buf, ("sub", "grp")))
        coarse_rounded = coarse.astype(jnp.bfloat16)
        solved = jnp.dot(schur_inv, scaled, preferred_element_type=jnp.float32)
        solved = solved + lax.dot_general(
            basis, coarse_rounded, (((0,), (0,)), ((), ())), preferred_element_type=jnp.float32
        )
        weighted = (scale_column * solved).astype(jnp.bfloat16)
        spread = (
            jnp.zeros((3 * own_count, weighted.shape[1]), jnp.bfloat16).at[source_row].set(weighted)
        )
        from_next = shifted(spread[:own_count], "sub", -1)
        from_previous = shifted(spread[2 * own_count :], "sub", 1)
        return (
            spread[own_count : 2 * own_count].astype(jnp.float32)
            + from_next.astype(jnp.float32)
            + from_previous.astype(jnp.float32)
        )

    first_apply = precondition(resid)
    second_apply = precondition(first_apply)
    return (first_apply, second_apply)


def solution(mesh):
    return jax.shard_map(
        shards,
        mesh=mesh,
        in_specs=(
            P(("sub", "grp"), None),
            P(("sub", "grp"), None),
            P(("sub", "grp"), None),
            P(("sub", "grp")),
            P(("sub", "grp"), None),
            P(("sub", "grp")),
            P(("sub", "grp")),
        ),
        out_specs=(P(("sub", "grp"), None), P(("sub", "grp"), None)),
        check_vma=False,
    )
```

profile of v0, /device:TPU:0, one launch (start us, length us, event | category | flops | bytes accessed | tf_op | source)
XLA Modules:
  0.0 418.4 jit_solution(4887360545982959692)
XLA Ops:
  7.2 0.0 copy-start
  7.2 0.0 all-reduce.3.cloned.1.call-start
  7.2 1.3 convert_element_type.56
  8.5 1.3 collective-permute-start.1
  9.8 5.5 %collective-permute-start = (bf16[1024,256]{1,0:T(8,128)(2,1)S(1)}, bf16[1024,256]{1,0:T(8,128)(2,1)S(1)}, u32[]{:S(2)}, u32[]{:S(2)}) collective-permute-start(bf16[1024,256]{1,0:T(8,128)(2,1)S(1)} %convert_element_type.56), channel_id=1, source_target_pairs={{0,4},{4,8},{8,12},{12,16},{16,20},{20,24},{24,28},{1,5},{5,9},{9,... | collective-permute-start | bytes 1572872 | tf_op jit(solution)/shard_map/ppermute | solution.py:15
  15.3 0.7 compare_select_fusion.1
  16.0 0.7 broadcast_clamp_fusion
  16.7 8.6 %collective-permute-done.1 = bf16[1024,256]{1,0:T(8,128)(2,1)S(1)} collective-permute-done((bf16[1024,256]{1,0:T(8,128)(2,1)S(1)}, bf16[1024,256]{1,0:T(8,128)(2,1)S(1)}, u32[]{:S(2)}, u32[]{:S(2)}) %collective-permute-start.1) | collective-permute-done | bytes 524320 | tf_op jit(solution)/shard_map/ppermute | solution.py:17
  25.3 11.4 %collective-permute-done = bf16[1024,256]{1,0:T(8,128)(2,1)S(1)} collective-permute-done((bf16[1024,256]{1,0:T(8,128)(2,1)S(1)}, bf16[1024,256]{1,0:T(8,128)(2,1)S(1)}, u32[]{:S(2)}, u32[]{:S(2)}) %collective-permute-start) | collective-permute-done | bytes 524320 | tf_op jit(solution)/shard_map/ppermute | solution.py:15
  36.7 0.1 pad_maximum_fusion
  36.8 7.5 %gather_fusion = bf16[2048,256]{1,0:T(8,128)(2,1)S(1)} fusion(bf16[3072,256]{1,0:T(8,128)(2,1)S(1)} %pad_maximum_fusion, s32[2048]{0:T(1024)S(1)} %get-tuple-element.8), kind=kCustom, calls=%fused_computation | custom fusion | bytes 2105344 | tf_op jit(solution)/shard_map/gather | solution.py:40
  44.3 0.3 multiply_convert_fusion.1
  44.6 0.6 gather_fusion.1
  45.3 0.7 copy-done.2
  46.0 0.0 all-reduce.3.cloned.1.call-update
  46.0 0.0 all-reduce.5.cloned.1.call-start
  46.1 5.8 %fusion.13 = f32[256,2048]{1,0:T(8,128)S(1)} fusion(bf16[2048,256]{1,0:T(8,128)(2,1)S(1)} %multiply_convert_fusion.1, bf16[2048,2048]{1,0:T(8,128)(2,1)} %param.8), kind=kOutput, calls=%fused_computation.35 | convolution fusion | flops 2147483648 | bytes 11534336 | tf_op jit(solution)/shard_map/dot_general | solution.py:50
  51.8 120.6 %all-reduce.3.cloned.1.call-done = bf16[512,256]{1,0:T(8,128)(2,1)} async-done(((bf16[512,256]{1,0:T(8,128)(2,1)}), bf16[512,256]{1,0:T(8,128)(2,1)}) %all-reduce.3.cloned.1.call-update) | async-done | bytes 262160 | tf_op jit(solution)/shard_map/psum | solution.py:48
  172.4 1.7 fusion.5
  174.1 0.5 copy.9
  174.6 9.8 %scatter_custom_fusion = bf16[3072,256]{1,0:T(8,128)(2,1)S(1)} fusion(s32[2048]{0:T(1024)S(1)} %get-tuple-element.9, bf16[2048,256]{1,0:T(8,128)(2,1)S(1)} %copy.9, bf16[]{:T(256)} %constant.10.clone.1), kind=kCustom, calls=%fused_computation.24 | custom fusion | bytes 1572866 | tf_op jit(solution)/shard_map/scatter | solution.py:56
  184.4 0.1 fusion.12
  184.5 1.3 collective-permute-start.2
  185.8 4.6 %collective-permute-start.3 = (bf16[1024,256]{1,0:T(8,128)(2,1)S(1)}, bf16[1024,256]{1,0:T(8,128)(2,1)S(1)}, u32[]{:S(2)}, u32[]{:S(2)}) collective-permute-start(bf16[1024,256]{1,0:T(8,128)(2,1)S(1)} %get-tuple-element.7), channel_id=1, source_target_pairs={{0,4},{4,8},{8,12},{12,16},{16,20},{20,24},{24,28},{1,5},{5,9},{9,... | collective-permute-start | bytes 1572872 | tf_op jit(solution)/shard_map/ppermute | solution.py:27
  190.4 8.9 %collective-permute-done.2 = bf16[1024,256]{1,0:T(8,128)(2,1)S(1)} collective-permute-done((bf16[1024,256]{1,0:T(8,128)(2,1)S(1)}, bf16[1024,256]{1,0:T(8,128)(2,1)S(1)}, u32[]{:S(2)}, u32[]{:S(2)}) %collective-permute-start.2) | collective-permute-done | bytes 524320 | tf_op jit(solution)/shard_map/ppermute | solution.py:27
  199.3 11.1 %collective-permute-done.3 = bf16[1024,256]{1,0:T(8,128)(2,1)S(1)} collective-permute-done((bf16[1024,256]{1,0:T(8,128)(2,1)S(1)}, bf16[1024,256]{1,0:T(8,128)(2,1)S(1)}, u32[]{:S(2)}, u32[]{:S(2)}) %collective-permute-start.3) | collective-permute-done | bytes 524320 | tf_op jit(solution)/shard_map/ppermute | solution.py:27
  210.4 1.2 fusion.10
  211.5 1.3 collective-permute-start.5
  212.8 5.2 %collective-permute-start.4 = (bf16[1024,256]{1,0:T(8,128)(2,1)S(1)}, bf16[1024,256]{1,0:T(8,128)(2,1)S(1)}, u32[]{:S(2)}, u32[]{:S(2)}) collective-permute-start(bf16[1024,256]{1,0:T(8,128)(2,1)S(1)} %get-tuple-element.2), channel_id=1, source_target_pairs={{0,4},{4,8},{8,12},{12,16},{16,20},{20,24},{24,28},{1,5},{5,9},{9,... | collective-permute-start | bytes 1572872 | tf_op jit(solution)/shard_map/ppermute | solution.py:15
  218.0 10.0 %collective-permute-done.5 = bf16[1024,256]{1,0:T(8,128)(2,1)S(1)} collective-permute-done((bf16[1024,256]{1,0:T(8,128)(2,1)S(1)}, bf16[1024,256]{1,0:T(8,128)(2,1)S(1)}, u32[]{:S(2)}, u32[]{:S(2)}) %collective-permute-start.5) | collective-permute-done | bytes 524320 | tf_op jit(solution)/shard_map/ppermute | solution.py:17
  228.0 11.4 %collective-permute-done.4 = bf16[1024,256]{1,0:T(8,128)(2,1)S(1)} collective-permute-done((bf16[1024,256]{1,0:T(8,128)(2,1)S(1)}, bf16[1024,256]{1,0:T(8,128)(2,1)S(1)}, u32[]{:S(2)}, u32[]{:S(2)}) %collective-permute-start.4) | collective-permute-done | bytes 524320 | tf_op jit(solution)/shard_map/ppermute | solution.py:15
  239.4 0.1 pad_maximum_fusion.1
  239.5 7.5 %gather_fusion.2 = bf16[2048,256]{1,0:T(8,128)(2,1)S(1)} fusion(bf16[3072,256]{1,0:T(8,128)(2,1)S(1)} %pad_maximum_fusion.1, s32[2048]{0:T(1024)S(1)} %get-tuple-element.8), kind=kCustom, calls=%fused_computation.2 | custom fusion | bytes 2105344 | tf_op jit(solution)/shard_map/gather | solution.py:40
  247.0 0.3 multiply_convert_fusion
  247.3 0.6 gather_fusion.3
  248.0 0.7 copy-done.1
  248.7 0.0 all-reduce.5.cloned.1.call-update
  248.7 5.8 %fusion.14 = f32[256,2048]{1,0:T(8,128)S(1)} fusion(bf16[2048,256]{1,0:T(8,128)(2,1)S(1)} %multiply_convert_fusion, bf16[2048,2048]{1,0:T(8,128)(2,1)} %param.8), kind=kOutput, calls=%fused_computation.36 | convolution fusion | flops 2147483648 | bytes 11534336 | tf_op jit(solution)/shard_map/dot_general | solution.py:50
  254.5 118.0 %all-reduce.5.cloned.1.call-done = bf16[512,256]{1,0:T(8,128)(2,1)} async-done(((bf16[512,256]{1,0:T(8,128)(2,1)}), bf16[512,256]{1,0:T(8,128)(2,1)}) %all-reduce.5.cloned.1.call-update) | async-done | bytes 262160 | tf_op jit(solution)/shard_map/psum | solution.py:48
  372.5 1.7 fusion.4
  374.1 0.5 copy.10
  374.7 9.8 %scatter_custom_fusion.1 = bf16[3072,256]{1,0:T(8,128)(2,1)S(1)} fusion(s32[2048]{0:T(1024)S(1)} %get-tuple-element.9, bf16[2048,256]{1,0:T(8,128)(2,1)S(1)} %copy.10, bf16[]{:T(256)} %constant.10.clone.1), kind=kCustom, calls=%fused_computation.22 | custom fusion | bytes 1572866 | tf_op jit(solution)/shard_map/scatter | solution.py:56
  384.5 0.1 fusion.11
  384.5 1.3 collective-permute-start.6
  385.8 4.6 %collective-permute-start.7 = (bf16[1024,256]{1,0:T(8,128)(2,1)S(1)}, bf16[1024,256]{1,0:T(8,128)(2,1)S(1)}, u32[]{:S(2)}, u32[]{:S(2)}) collective-permute-start(bf16[1024,256]{1,0:T(8,128)(2,1)S(1)} %get-tuple-element.5), channel_id=1, source_target_pairs={{0,4},{4,8},{8,12},{12,16},{16,20},{20,24},{24,28},{1,5},{5,9},{9,... | collective-permute-start | bytes 1572872 | tf_op jit(solution)/shard_map/ppermute | solution.py:27
  390.4 8.9 %collective-permute-done.6 = bf16[1024,256]{1,0:T(8,128)(2,1)S(1)} collective-permute-done((bf16[1024,256]{1,0:T(8,128)(2,1)S(1)}, bf16[1024,256]{1,0:T(8,128)(2,1)S(1)}, u32[]{:S(2)}, u32[]{:S(2)}) %collective-permute-start.6) | collective-permute-done | bytes 524320 | tf_op jit(solution)/shard_map/ppermute | solution.py:27
  399.3 11.1 %collective-permute-done.7 = bf16[1024,256]{1,0:T(8,128)(2,1)S(1)} collective-permute-done((bf16[1024,256]{1,0:T(8,128)(2,1)S(1)}, bf16[1024,256]{1,0:T(8,128)(2,1)S(1)}, u32[]{:S(2)}, u32[]{:S(2)}) %collective-permute-start.7) | collective-permute-done | bytes 524320 | tf_op jit(solution)/shard_map/ppermute | solution.py:27
  410.4 1.1 convert_add_fusion
  (12 shorter events, 0.1 us)
Async XLA Ops:
  7.2 165.2 %copy-start = (bf16[16,2048]{1,0:T(8,128)(2,1)S(1)}, bf16[16,2048]{1,0:T(8,128)(2,1)}, u32[]{:S(2)}) copy-start(bf16[16,2048]{1,0:T(8,128)(2,1)} %param.9) | copy-start | bytes 196612
  7.2 165.2 %all-reduce.3.cloned.1.call-start = ((), (), s32[]{:S(2)}) async-start(), calls=%async_computation | async-start | bytes 524288 | tf_op jit(solution)/shard_map/psum | solution.py:48
  8.5 16.8 %collective-permute-start.1 = (bf16[1024,256]{1,0:T(8,128)(2,1)S(1)}, bf16[1024,256]{1,0:T(8,128)(2,1)S(1)}, u32[]{:S(2)}, u32[]{:S(2)}) collective-permute-start(bf16[1024,256]{1,0:T(8,128)(2,1)S(1)} %convert_element_type.56), channel_id=1, source_target_pairs={{4,0},{8,4},{12,8},{16,12},{20,16},{24,20},{28,24},{5,1},{9,5},{13... | collective-permute-start | bytes 1572872 | tf_op jit(solution)/shard_map/ppermute | solution.py:17
  9.8 26.8 %collective-permute-start = (bf16[1024,256]{1,0:T(8,128)(2,1)S(1)}, bf16[1024,256]{1,0:T(8,128)(2,1)S(1)}, u32[]{:S(2)}, u32[]{:S(2)}) collective-permute-start(bf16[1024,256]{1,0:T(8,128)(2,1)S(1)} %convert_element_type.56), channel_id=1, source_target_pairs={{0,4},{4,8},{8,12},{12,16},{16,20},{20,24},{24,28},{1,5},{5,9},{9,... | collective-permute-start | bytes 1572872 | tf_op jit(solution)/shard_map/ppermute | solution.py:15
  36.8 7.5 %copy-start.3 = (f32[2048]{0:T(1024)S(1)}, f32[2048]{0:T(1024)}, u32[]{:S(2)}) copy-start(f32[2048]{0:T(1024)} %param.10) | copy-start | bytes 24580
  45.3 0.7 copy-start.2
  46.0 126.4 %copy-start.4 = (bf16[16,512]{1,0:T(8,128)(2,1)S(1)}, bf16[16,512]{1,0:T(8,128)(2,1)}, u32[]{:S(2)}) copy-start(bf16[16,512]{1,0:T(8,128)(2,1)} %param.11) | copy-start | bytes 49156
  46.0 326.5 %all-reduce.5.cloned.1.call-start = ((), (), s32[]{:S(2)}) async-start(), calls=%async_computation.1 | async-start | bytes 524288 | tf_op jit(solution)/shard_map/psum | solution.py:48
  184.5 14.8 %collective-permute-start.2 = (bf16[1024,256]{1,0:T(8,128)(2,1)S(1)}, bf16[1024,256]{1,0:T(8,128)(2,1)S(1)}, u32[]{:S(2)}, u32[]{:S(2)}) collective-permute-start(bf16[1024,256]{1,0:T(8,128)(2,1)S(1)} %get-tuple-element.6), channel_id=1, source_target_pairs={{4,0},{8,4},{12,8},{16,12},{20,16},{24,20},{28,24},{5,1},{9,5},{13... | collective-permute-start | bytes 1572872 | tf_op jit(solution)/shard_map/ppermute | solution.py:27
  185.8 24.6 %collective-permute-start.3 = (bf16[1024,256]{1,0:T(8,128)(2,1)S(1)}, bf16[1024,256]{1,0:T(8,128)(2,1)S(1)}, u32[]{:S(2)}, u32[]{:S(2)}) collective-permute-start(bf16[1024,256]{1,0:T(8,128)(2,1)S(1)} %get-tuple-element.7), channel_id=1, source_target_pairs={{0,4},{4,8},{8,12},{12,16},{16,20},{20,24},{24,28},{1,5},{5,9},{9,... | collective-permute-start | bytes 1572872 | tf_op jit(solution)/shard_map/ppermute | solution.py:27
  211.5 16.5 %collective-permute-start.5 = (bf16[1024,256]{1,0:T(8,128)(2,1)S(1)}, bf16[1024,256]{1,0:T(8,128)(2,1)S(1)}, u32[]{:S(2)}, u32[]{:S(2)}) collective-permute-start(bf16[1024,256]{1,0:T(8,128)(2,1)S(1)} %get-tuple-element.2), channel_id=1, source_target_pairs={{4,0},{8,4},{12,8},{16,12},{20,16},{24,20},{28,24},{5,1},{9,5},{13... | collective-permute-start | bytes 1572872 | tf_op jit(solution)/shard_map/ppermute | solution.py:17
  212.8 26.6 %collective-permute-start.4 = (bf16[1024,256]{1,0:T(8,128)(2,1)S(1)}, bf16[1024,256]{1,0:T(8,128)(2,1)S(1)}, u32[]{:S(2)}, u32[]{:S(2)}) collective-permute-start(bf16[1024,256]{1,0:T(8,128)(2,1)S(1)} %get-tuple-element.2), channel_id=1, source_target_pairs={{0,4},{4,8},{8,12},{12,16},{16,20},{20,24},{24,28},{1,5},{5,9},{9,... | collective-permute-start | bytes 1572872 | tf_op jit(solution)/shard_map/ppermute | solution.py:15
  248.0 0.7 copy-start.1
  384.5 14.8 %collective-permute-start.6 = (bf16[1024,256]{1,0:T(8,128)(2,1)S(1)}, bf16[1024,256]{1,0:T(8,128)(2,1)S(1)}, u32[]{:S(2)}, u32[]{:S(2)}) collective-permute-start(bf16[1024,256]{1,0:T(8,128)(2,1)S(1)} %get-tuple-element.4), channel_id=1, source_target_pairs={{4,0},{8,4},{12,8},{16,12},{20,16},{24,20},{28,24},{5,1},{9,5},{13... | collective-permute-start | bytes 1572872 | tf_op jit(solution)/shard_map/ppermute | solution.py:27
  385.8 24.6 %collective-permute-start.7 = (bf16[1024,256]{1,0:T(8,128)(2,1)S(1)}, bf16[1024,256]{1,0:T(8,128)(2,1)S(1)}, u32[]{:S(2)}, u32[]{:S(2)}) collective-permute-start(bf16[1024,256]{1,0:T(8,128)(2,1)S(1)} %get-tuple-element.5), channel_id=1, source_target_pairs={{0,4},{4,8},{8,12},{12,16},{16,20},{20,24},{24,28},{1,5},{5,9},{9,... | collective-permute-start | bytes 1572872 | tf_op jit(solution)/shard_map/ppermute | solution.py:27
Sparse Core Ops, SparseCore 0:
  46.1 126.2 all-reduce.2
  248.8 123.6 all-reduce.4
where the time goes:
time: 419 us; the launch traced here: 418 us
  waiting for transfers between devices  320 us (76%)
  local copies, waits for them, and re-layouts  38.4 us (9%)
  starting transfers between devices  25.1 us (6%)
  matrix products  14.9 us (4%)
  between operations  14.3 us (3%)
  other arithmetic  5.82 us (1%)
    psum x2, waiting for transfers between devices, precondition(): coarse = add_all(lax.psum(buf, ('sub', 'grp')))  239 us
    ppermute x4, waiting for transfers between devices, shifted(): return lax.ppermute(shard, axis, pairs)  40 us
    ppermute x2, waiting for transfers between devices, with_halo(): lax.ppermute(tail, axis, [(i, (i + 1) % count) for i in range(ends)])  22.8 us
    scatter x2, local copies, waits for them, and re-layouts, precondition(): jnp.zeros((3 * own_count, weighted.shape[1]), jnp.bfloat16).at[source_row]  19.6 us
    ppermute x2, waiting for transfers between devices, with_halo(): lax.ppermute(head, axis, [((i + 1) % count, i) for i in range(ends)])  18.5 us
    gather x2, local copies, waits for them, and re-layouts, precondition(): gathered = padded[source_row]  15 us
    ppermute x4, starting transfers between devices, shifted(): return lax.ppermute(shard, axis, pairs)  11.7 us
    dot_general x2, matrix products, precondition(): solved = jnp.dot(schur_inv, scaled, preferred_element_type=jnp.float32)  11.5 us
  transfers between devices with their start and end apart: 10, of which 10 were waited for; matrix products, arithmetic and copies ran while one was open for 3% of the time, Pallas kernels for 0%

commit v1 on v0

--- a/solution.py
+++ b/solution.py
@@ -45,7 +45,7 @@
         buf = lax.dynamic_update_slice(
             jnp.zeros((total, primal.shape[1]), primal.dtype), primal, (idx * primal.shape[0], 0)
         )
-        coarse = add_all(lax.psum(buf, ("sub", "grp")))
+        coarse = add_all(jnp.sum(lax.all_gather(buf, ("sub", "grp")), axis=0))
         coarse_rounded = coarse.astype(jnp.bfloat16)
         solved = jnp.dot(schur_inv, scaled, preferred_element_type=jnp.float32)
         solved = solved + lax.dot_general(

time: 419 us -> 335 us (0.80)
  waiting for transfers between devices: 320 us -> 228 us
  other arithmetic: 5.82 us -> 15.3 us
    psum x2 -> x0, waiting for transfers between devices: 239 us -> none  [precondition(): coarse = add_all(lax.psum(buf, ('sub', 'grp')))]
    all_gather x0 -> x2, waiting for transfers between devices: none -> 145 us  [precondition(): coarse = add_all(jnp.sum(lax.all_gather(buf, ('sub', 'grp')), axis=0))]
    reduce_sum x0 -> x2, other arithmetic: none -> 9.5 us  [precondition(): coarse = add_all(jnp.sum(lax.all_gather(buf, ('sub', 'grp')), axis=0))]
  transfers between devices with their start and end apart: 10 -> 10, of which waited for: 10 -> 10; matrix products, arithmetic and copies ran while one was open for 3% -> 4% of each run, Pallas kernels for 0% -> 0%
where the time goes in v1:
time: 335 us
  waiting for transfers between devices  228 us (68%)
  local copies, waits for them, and re-layouts  38.4 us (11%)
  starting transfers between devices  25.1 us (7%)
  other arithmetic  15.3 us (5%)
  between operations  14.3 us (4%)
  matrix products  13 us (4%)
    all_gather x2, waiting for transfers between devices, precondition(): coarse = add_all(jnp.sum(lax.all_gather(buf, ('sub', 'grp')), axis=0))  145 us
    ppermute x4, waiting for transfers between devices, shifted(): return lax.ppermute(shard, axis, pairs)  42.4 us
    ppermute x2, waiting for transfers between devices, with_halo(): lax.ppermute(tail, axis, [(i, (i + 1) % count) for i in range(ends)])  22.8 us
    scatter x2, local copies, waits for them, and re-layouts, precondition(): jnp.zeros((3 * own_count, weighted.shape[1]), jnp.bfloat16).at[source_row]  19.6 us
    ppermute x2, waiting for transfers between devices, with_halo(): lax.ppermute(head, axis, [((i + 1) % count, i) for i in range(ends)])  18.5 us
    gather x2, local copies, waits for them, and re-layouts, precondition(): gathered = padded[source_row]  15 us
    ppermute x4, starting transfers between devices, shifted(): return lax.ppermute(shard, axis, pairs)  11.7 us
    dot_general x2, matrix products, precondition(): solved = jnp.dot(schur_inv, scaled, preferred_element_type=jnp.float32)  11.5 us
  transfers between devices with their start and end apart: 10, of which 10 were waited for; matrix products, arithmetic and copies ran while one was open for 4% of the time, Pallas kernels for 0%

profile of v1, /device:TPU:0, one launch (start us, length us, event | category | flops | bytes accessed | tf_op | source)
XLA Modules:
  0.0 334.5 jit_solution(5866729613659919513)
XLA Ops:
  7.2 0.0 all-gather.3.cloned.1.call-start
  7.2 1.3 convert_element_type.60
  8.5 1.3 collective-permute-start.1
  9.8 5.5 %collective-permute-start = (bf16[1024,256]{1,0:T(8,128)(2,1)S(1)}, bf16[1024,256]{1,0:T(8,128)(2,1)S(1)}, u32[]{:S(2)}, u32[]{:S(2)}) collective-permute-start(bf16[1024,256]{1,0:T(8,128)(2,1)S(1)} %convert_element_type.60), channel_id=1, source_target_pairs={{0,4},{4,8},{8,12},{12,16},{16,20},{20,24},{24,28},{1,5},{5,9},{9,... | collective-permute-start | bytes 1572872 | tf_op jit(solution)/shard_map/ppermute | solution.py:15
  15.3 0.7 compare_select_fusion.1
  16.0 0.7 broadcast_clamp_fusion
  16.7 8.6 %collective-permute-done.1 = bf16[1024,256]{1,0:T(8,128)(2,1)S(1)} collective-permute-done((bf16[1024,256]{1,0:T(8,128)(2,1)S(1)}, bf16[1024,256]{1,0:T(8,128)(2,1)S(1)}, u32[]{:S(2)}, u32[]{:S(2)}) %collective-permute-start.1) | collective-permute-done | bytes 524320 | tf_op jit(solution)/shard_map/ppermute | solution.py:17
  25.3 11.4 %collective-permute-done = bf16[1024,256]{1,0:T(8,128)(2,1)S(1)} collective-permute-done((bf16[1024,256]{1,0:T(8,128)(2,1)S(1)}, bf16[1024,256]{1,0:T(8,128)(2,1)S(1)}, u32[]{:S(2)}, u32[]{:S(2)}) %collective-permute-start) | collective-permute-done | bytes 524320 | tf_op jit(solution)/shard_map/ppermute | solution.py:15
  36.7 0.1 pad_maximum_fusion
  36.8 7.5 %gather_fusion = bf16[2048,256]{1,0:T(8,128)(2,1)S(1)} fusion(bf16[3072,256]{1,0:T(8,128)(2,1)S(1)} %pad_maximum_fusion, s32[2048]{0:T(1024)S(1)} %get-tuple-element.8), kind=kCustom, calls=%fused_computation | custom fusion | bytes 2105344 | tf_op jit(solution)/shard_map/gather | solution.py:40
  44.3 0.3 multiply_convert_fusion.1
  44.6 0.6 gather_fusion.1
  45.3 0.7 copy-done.2
  46.0 0.0 all-gather.3.cloned.1.call-update
  46.0 0.0 all-gather.5.cloned.1.call-start
  46.0 5.8 %fusion.13 = f32[256,2048]{1,0:T(8,128)S(1)} fusion(bf16[2048,256]{1,0:T(8,128)(2,1)S(1)} %multiply_convert_fusion.1, bf16[2048,2048]{1,0:T(8,128)(2,1)} %param.8), kind=kOutput, calls=%fused_computation.35 | convolution fusion | flops 2147483648 | bytes 11534336 | tf_op jit(solution)/shard_map/dot_general | solution.py:50
  51.8 73.1 %all-gather.3.cloned.1.call-done = bf16[32,512,256]{2,1,0:T(8,128)(2,1)} async-done(((bf16[1,512,256]{2,1,0:T(8,128)(2,1)}), bf16[32,512,256]{2,1,0:T(8,128)(2,1)}) %all-gather.3.cloned.1.call-update) | async-done | bytes 8388624 | tf_op jit(solution)/shard_map/all_gather | solution.py:48
  124.9 4.7 %reduce_sum.24 = bf16[512,256]{1,0:T(8,128)(2,1)S(1)} reduce(bf16[32,512,256]{2,1,0:T(8,128)(2,1)} %all-gather.3.cloned.1.call-done, bf16[]{:T(256)} %constant.10.clone.1), dimensions={0}, to_apply=%region_0.0 | reduce | flops 4063232 | bytes 8650754 | tf_op jit(solution)/shard_map/reduce_sum | solution.py:48
  129.7 0.7 fusion.5
  130.4 0.5 copy.11
  131.0 9.8 %scatter_custom_fusion = bf16[3072,256]{1,0:T(8,128)(2,1)S(1)} fusion(s32[2048]{0:T(1024)S(1)} %get-tuple-element.9, bf16[2048,256]{1,0:T(8,128)(2,1)S(1)} %copy.11, bf16[]{:T(256)} %constant.10.clone.1), kind=kCustom, calls=%fused_computation.24 | custom fusion | bytes 1572866 | tf_op jit(solution)/shard_map/scatter | solution.py:56
  140.8 0.1 fusion.12
  140.8 1.3 collective-permute-start.2
  142.1 4.6 %collective-permute-start.3 = (bf16[1024,256]{1,0:T(8,128)(2,1)S(1)}, bf16[1024,256]{1,0:T(8,128)(2,1)S(1)}, u32[]{:S(2)}, u32[]{:S(2)}) collective-permute-start(bf16[1024,256]{1,0:T(8,128)(2,1)S(1)} %get-tuple-element.7), channel_id=1, source_target_pairs={{0,4},{4,8},{8,12},{12,16},{16,20},{20,24},{24,28},{1,5},{5,9},{9,... | collective-permute-start | bytes 1572872 | tf_op jit(solution)/shard_map/ppermute | solution.py:27
  146.7 10.1 %collective-permute-done.2 = bf16[1024,256]{1,0:T(8,128)(2,1)S(1)} collective-permute-done((bf16[1024,256]{1,0:T(8,128)(2,1)S(1)}, bf16[1024,256]{1,0:T(8,128)(2,1)S(1)}, u32[]{:S(2)}, u32[]{:S(2)}) %collective-permute-start.2) | collective-permute-done | bytes 524320 | tf_op jit(solution)/shard_map/ppermute | solution.py:27
  156.8 11.1 %collective-permute-done.3 = bf16[1024,256]{1,0:T(8,128)(2,1)S(1)} collective-permute-done((bf16[1024,256]{1,0:T(8,128)(2,1)S(1)}, bf16[1024,256]{1,0:T(8,128)(2,1)S(1)}, u32[]{:S(2)}, u32[]{:S(2)}) %collective-permute-start.3) | collective-permute-done | bytes 524320 | tf_op jit(solution)/shard_map/ppermute | solution.py:27
  167.9 1.2 fusion.10
  169.1 1.3 collective-permute-start.5
  170.3 5.2 %collective-permute-start.4 = (bf16[1024,256]{1,0:T(8,128)(2,1)S(1)}, bf16[1024,256]{1,0:T(8,128)(2,1)S(1)}, u32[]{:S(2)}, u32[]{:S(2)}) collective-permute-start(bf16[1024,256]{1,0:T(8,128)(2,1)S(1)} %get-tuple-element.2), channel_id=1, source_target_pairs={{0,4},{4,8},{8,12},{12,16},{16,20},{20,24},{24,28},{1,5},{5,9},{9,... | collective-permute-start | bytes 1572872 | tf_op jit(solution)/shard_map/ppermute | solution.py:15
  175.6 10.0 %collective-permute-done.5 = bf16[1024,256]{1,0:T(8,128)(2,1)S(1)} collective-permute-done((bf16[1024,256]{1,0:T(8,128)(2,1)S(1)}, bf16[1024,256]{1,0:T(8,128)(2,1)S(1)}, u32[]{:S(2)}, u32[]{:S(2)}) %collective-permute-start.5) | collective-permute-done | bytes 524320 | tf_op jit(solution)/shard_map/ppermute | solution.py:17
  185.5 11.4 %collective-permute-done.4 = bf16[1024,256]{1,0:T(8,128)(2,1)S(1)} collective-permute-done((bf16[1024,256]{1,0:T(8,128)(2,1)S(1)}, bf16[1024,256]{1,0:T(8,128)(2,1)S(1)}, u32[]{:S(2)}, u32[]{:S(2)}) %collective-permute-start.4) | collective-permute-done | bytes 524320 | tf_op jit(solution)/shard_map/ppermute | solution.py:15
  196.9 0.1 pad_maximum_fusion.1
  197.0 7.5 %gather_fusion.2 = bf16[2048,256]{1,0:T(8,128)(2,1)S(1)} fusion(bf16[3072,256]{1,0:T(8,128)(2,1)S(1)} %pad_maximum_fusion.1, s32[2048]{0:T(1024)S(1)} %get-tuple-element.8), kind=kCustom, calls=%fused_computation.2 | custom fusion | bytes 2105344 | tf_op jit(solution)/shard_map/gather | solution.py:40
  204.5 0.3 multiply_convert_fusion
  204.9 0.6 gather_fusion.3
  205.5 0.7 copy-done.1
  206.2 5.8 %fusion.14 = f32[256,2048]{1,0:T(8,128)S(1)} fusion(bf16[2048,256]{1,0:T(8,128)(2,1)S(1)} %multiply_convert_fusion, bf16[2048,2048]{1,0:T(8,128)(2,1)} %param.8), kind=kOutput, calls=%fused_computation.36 | convolution fusion | flops 2147483648 | bytes 11534336 | tf_op jit(solution)/shard_map/dot_general | solution.py:50
  212.0 71.6 %all-gather.5.cloned.1.call-done = bf16[32,512,256]{2,1,0:T(8,128)(2,1)} async-done(((bf16[1,512,256]{2,1,0:T(8,128)(2,1)}), bf16[32,512,256]{2,1,0:T(8,128)(2,1)}) %all-gather.5.cloned.1.call-update) | async-done | bytes 8388624 | tf_op jit(solution)/shard_map/all_gather | solution.py:48
  283.6 4.7 %reduce_sum.25 = bf16[512,256]{1,0:T(8,128)(2,1)S(1)} reduce(bf16[32,512,256]{2,1,0:T(8,128)(2,1)} %all-gather.5.cloned.1.call-done, bf16[]{:T(256)} %constant.10.clone.1), dimensions={0}, to_apply=%region_2.0 | reduce | flops 4063232 | bytes 8650754 | tf_op jit(solution)/shard_map/reduce_sum | solution.py:48
  288.3 0.7 fusion.4
  289.1 0.5 copy.12
  289.6 9.8 %scatter_custom_fusion.1 = bf16[3072,256]{1,0:T(8,128)(2,1)S(1)} fusion(s32[2048]{0:T(1024)S(1)} %get-tuple-element.9, bf16[2048,256]{1,0:T(8,128)(2,1)S(1)} %copy.12, bf16[]{:T(256)} %constant.10.clone.1), kind=kCustom, calls=%fused_computation.22 | custom fusion | bytes 1572866 | tf_op jit(solution)/shard_map/scatter | solution.py:56
  299.4 0.1 fusion.11
  299.5 1.3 collective-permute-start.6
  300.8 4.6 %collective-permute-start.7 = (bf16[1024,256]{1,0:T(8,128)(2,1)S(1)}, bf16[1024,256]{1,0:T(8,128)(2,1)S(1)}, u32[]{:S(2)}, u32[]{:S(2)}) collective-permute-start(bf16[1024,256]{1,0:T(8,128)(2,1)S(1)} %get-tuple-element.5), channel_id=1, source_target_pairs={{0,4},{4,8},{8,12},{12,16},{16,20},{20,24},{24,28},{1,5},{5,9},{9,... | collective-permute-start | bytes 1572872 | tf_op jit(solution)/shard_map/ppermute | solution.py:27
  305.4 10.1 %collective-permute-done.6 = bf16[1024,256]{1,0:T(8,128)(2,1)S(1)} collective-permute-done((bf16[1024,256]{1,0:T(8,128)(2,1)S(1)}, bf16[1024,256]{1,0:T(8,128)(2,1)S(1)}, u32[]{:S(2)}, u32[]{:S(2)}) %collective-permute-start.6) | collective-permute-done | bytes 524320 | tf_op jit(solution)/shard_map/ppermute | solution.py:27
  315.5 11.1 %collective-permute-done.7 = bf16[1024,256]{1,0:T(8,128)(2,1)S(1)} collective-permute-done((bf16[1024,256]{1,0:T(8,128)(2,1)S(1)}, bf16[1024,256]{1,0:T(8,128)(2,1)S(1)}, u32[]{:S(2)}, u32[]{:S(2)}) %collective-permute-start.7) | collective-permute-done | bytes 524320 | tf_op jit(solution)/shard_map/ppermute | solution.py:27
  326.5 1.1 convert_add_fusion
  (14 shorter events, 0.1 us)
Async XLA Ops:
  7.2 122.5 %copy-start = (bf16[16,2048]{1,0:T(8,128)(2,1)S(1)}, bf16[16,2048]{1,0:T(8,128)(2,1)}, u32[]{:S(2)}) copy-start(bf16[16,2048]{1,0:T(8,128)(2,1)} %param.9) | copy-start | bytes 196612
  7.2 117.8 %all-gather.3.cloned.1.call-start = ((), (), s32[]{:S(2)}) async-start(), calls=%async_computation | async-start | bytes 8650752 | tf_op jit(solution)/shard_map/all_gather | solution.py:48
  8.5 16.8 %collective-permute-start.1 = (bf16[1024,256]{1,0:T(8,128)(2,1)S(1)}, bf16[1024,256]{1,0:T(8,128)(2,1)S(1)}, u32[]{:S(2)}, u32[]{:S(2)}) collective-permute-start(bf16[1024,256]{1,0:T(8,128)(2,1)S(1)} %convert_element_type.60), channel_id=1, source_target_pairs={{4,0},{8,4},{12,8},{16,12},{20,16},{24,20},{28,24},{5,1},{9,5},{13... | collective-permute-start | bytes 1572872 | tf_op jit(solution)/shard_map/ppermute | solution.py:17
  9.8 26.8 %collective-permute-start = (bf16[1024,256]{1,0:T(8,128)(2,1)S(1)}, bf16[1024,256]{1,0:T(8,128)(2,1)S(1)}, u32[]{:S(2)}, u32[]{:S(2)}) collective-permute-start(bf16[1024,256]{1,0:T(8,128)(2,1)S(1)} %convert_element_type.60), channel_id=1, source_target_pairs={{0,4},{4,8},{8,12},{12,16},{16,20},{20,24},{24,28},{1,5},{5,9},{9,... | collective-permute-start | bytes 1572872 | tf_op jit(solution)/shard_map/ppermute | solution.py:15
  36.8 7.5 %copy-start.3 = (f32[2048]{0:T(1024)S(1)}, f32[2048]{0:T(1024)}, u32[]{:S(2)}) copy-start(f32[2048]{0:T(1024)} %param.10) | copy-start | bytes 24580
  45.3 0.7 copy-start.2
  46.0 237.6 %all-gather.5.cloned.1.call-start = ((), (), s32[]{:S(2)}) async-start(), calls=%async_computation.1 | async-start | bytes 8650752 | tf_op jit(solution)/shard_map/all_gather | solution.py:48
  51.8 77.9 %copy-start.4 = (bf16[16,512]{1,0:T(8,128)(2,1)S(1)}, bf16[16,512]{1,0:T(8,128)(2,1)}, u32[]{:S(2)}) copy-start(bf16[16,512]{1,0:T(8,128)(2,1)} %param.11) | copy-start | bytes 49156
  140.8 16.0 %collective-permute-start.2 = (bf16[1024,256]{1,0:T(8,128)(2,1)S(1)}, bf16[1024,256]{1,0:T(8,128)(2,1)S(1)}, u32[]{:S(2)}, u32[]{:S(2)}) collective-permute-start(bf16[1024,256]{1,0:T(8,128)(2,1)S(1)} %get-tuple-element.6), channel_id=1, source_target_pairs={{4,0},{8,4},{12,8},{16,12},{20,16},{24,20},{28,24},{5,1},{9,5},{13... | collective-permute-start | bytes 1572872 | tf_op jit(solution)/shard_map/ppermute | solution.py:27
  142.1 25.8 %collective-permute-start.3 = (bf16[1024,256]{1,0:T(8,128)(2,1)S(1)}, bf16[1024,256]{1,0:T(8,128)(2,1)S(1)}, u32[]{:S(2)}, u32[]{:S(2)}) collective-permute-start(bf16[1024,256]{1,0:T(8,128)(2,1)S(1)} %get-tuple-element.7), channel_id=1, source_target_pairs={{0,4},{4,8},{8,12},{12,16},{16,20},{20,24},{24,28},{1,5},{5,9},{9,... | collective-permute-start | bytes 1572872 | tf_op jit(solution)/shard_map/ppermute | solution.py:27
  169.1 16.5 %collective-permute-start.5 = (bf16[1024,256]{1,0:T(8,128)(2,1)S(1)}, bf16[1024,256]{1,0:T(8,128)(2,1)S(1)}, u32[]{:S(2)}, u32[]{:S(2)}) collective-permute-start(bf16[1024,256]{1,0:T(8,128)(2,1)S(1)} %get-tuple-element.2), channel_id=1, source_target_pairs={{4,0},{8,4},{12,8},{16,12},{20,16},{24,20},{28,24},{5,1},{9,5},{13... | collective-permute-start | bytes 1572872 | tf_op jit(solution)/shard_map/ppermute | solution.py:17
  170.3 26.6 %collective-permute-start.4 = (bf16[1024,256]{1,0:T(8,128)(2,1)S(1)}, bf16[1024,256]{1,0:T(8,128)(2,1)S(1)}, u32[]{:S(2)}, u32[]{:S(2)}) collective-permute-start(bf16[1024,256]{1,0:T(8,128)(2,1)S(1)} %get-tuple-element.2), channel_id=1, source_target_pairs={{0,4},{4,8},{8,12},{12,16},{16,20},{20,24},{24,28},{1,5},{5,9},{9,... | collective-permute-start | bytes 1572872 | tf_op jit(solution)/shard_map/ppermute | solution.py:15
  205.5 0.7 copy-start.1
  299.5 16.0 %collective-permute-start.6 = (bf16[1024,256]{1,0:T(8,128)(2,1)S(1)}, bf16[1024,256]{1,0:T(8,128)(2,1)S(1)}, u32[]{:S(2)}, u32[]{:S(2)}) collective-permute-start(bf16[1024,256]{1,0:T(8,128)(2,1)S(1)} %get-tuple-element.4), channel_id=1, source_target_pairs={{4,0},{8,4},{12,8},{16,12},{20,16},{24,20},{28,24},{5,1},{9,5},{13... | collective-permute-start | bytes 1572872 | tf_op jit(solution)/shard_map/ppermute | solution.py:27
  300.8 25.8 %collective-permute-start.7 = (bf16[1024,256]{1,0:T(8,128)(2,1)S(1)}, bf16[1024,256]{1,0:T(8,128)(2,1)S(1)}, u32[]{:S(2)}, u32[]{:S(2)}) collective-permute-start(bf16[1024,256]{1,0:T(8,128)(2,1)S(1)} %get-tuple-element.5), channel_id=1, source_target_pairs={{0,4},{4,8},{8,12},{12,16},{16,20},{20,24},{24,28},{1,5},{5,9},{9,... | collective-permute-start | bytes 1572872 | tf_op jit(solution)/shard_map/ppermute | solution.py:27
Sparse Core Ops, SparseCore 0:
  46.1 78.7 all-gather.2
  206.4 77.1 all-gather.4
